TPU v7x, 32 devices: a whole 2x2x4 slice. The times are simulated.
32 devices in a mesh: groups: 2 (over y), tm: 4 (over z), mp: 2 (over x), section: 2 (over core).
Axes of the slice: x: 2, y: 2, z: 4, core: 2. Of those that a mesh axis runs over, the one named last changes fastest.
Arguments:
- series: bfloat16 [4, 64, 16384], P('groups', None, 'tm'), parts along dimension 0, may hold values from -80 to 80
- lengths: int32 [4], P('groups'), parts along dimension 0, may hold values from 2048 to 16384, as said below
- patch_weight: bfloat16 [4096, 1280], P(None, ('mp', 'section')), may hold values from -0.09375 to 0.09375
- norm_gain: bfloat16 [2, 1280], P('section'), may hold values from 0.099609375 to 1.8984375
- query_weight: bfloat16 [2, 1280, 1280], P('section', None, 'mp'), may hold values from -4 to 4
- key_weight: bfloat16 [2, 1280, 320], P('section', None, 'mp'), may hold values from -4 to 4
- value_weight: bfloat16 [2, 1280, 320], P('section', None, 'mp'), may hold values from -0.15625 to 0.15625
- out_weight: bfloat16 [2, 1280, 1280], P('section', 'mp'), may hold values from -0.625 to 0.625
Outputs:
- key_cache: bfloat16 [2, 4, 4, 80, 512], P('section', 'groups', 'mp', None, 'tm'), parts along dimension 1
- value_cache: bfloat16 [2, 4, 4, 80, 512], P('section', 'groups', 'mp', None, 'tm'), parts along dimension 1
- hidden: bfloat16 [4, 512, 1280], P(('groups', 'section'), 'tm', 'mp'), parts along dimension 0
There are 2 independent parts, one for each index of `groups`. A program takes and returns all parts, laid end to end along the dimension named above; an argument that names none is the same for every part. Nothing has to cross between parts.
Inputs may be any that keep to these rules, and one draw needn't show every extreme that they name: `lengths`: a multiple of 32; the last sequence of a part has its whole history of 16384 steps.
All inputs are finite; a program needn't handle non-finite values.
Results may differ from a plain program's by a relative error of at most 0.02.
Values may be sent and summed in bfloat16 or wider, within the bound.
No kernel may reach another device: no remote copies, remote signals or barrier semaphores. Data moves between devices by JAX's collectives and lax.ppermute only.
A program may use at most 64 MiB of HBM per device.

v0:
```python
import jax
import jax.numpy as jnp
from jax import lax
from jax.sharding import PartitionSpec as P

STRIDE = 32
HD = 80


def from_behind(value, axis, by):
    size = lax.axis_size(axis)
    pairs = [(i, i + by) for i in range(size) if 0 <= i + by < size]
    return lax.ppermute(value, axis, pairs)


def from_root(value, axis, root):
    mine = lax.axis_index(axis) == root
    return lax.psum(jnp.where(mine, value, jnp.zeros_like(value)), axis)


def absorb_block(running, key_block, value_block, key_start, query_rows, query_pos, first_valid):
    run_max, run_sum, accumulated = running
    key_pos = key_start + jnp.arange(key_block.shape[3], dtype=jnp.int32)
    allowed = (key_pos[None, None, :] <= query_pos[None, :, None]) & (
        (key_pos[None, None, :] >= first_valid[:, None, None])
        | (key_pos[None, None, :] == query_pos[None, :, None])
    )
    scores = jnp.einsum(
        "btkgh,bkhn->bkgtn", query_rows, key_block, preferred_element_type=jnp.float32
    )
    scores = jnp.where(allowed[:, None, None], scores, -jnp.inf)
    new_max = jnp.maximum(run_max, jnp.max(scores, -1))
    rescale = jnp.exp(run_max - new_max)
    exp_scores = jnp.exp(scores - new_max[..., None])
    new_sum = run_sum * rescale + jnp.sum(exp_scores, -1)
    contribution = jnp.einsum(
        "bkgtn,bkhn->bkgth",
        exp_scores.astype(jnp.bfloat16),
        value_block,
        preferred_element_type=jnp.float32,
    )
    return (new_max, new_sum, accumulated * rescale[..., None] + contribution)


def attend_layer(
    hidden_in, seq_lens, gain, query_w, key_w, value_w, out_w, tok_start, total_tokens
):
    batch_count, tok_count, share_width = hidden_in.shape
    hidden32 = hidden_in.astype(jnp.float32)
    gain32 = gain.astype(jnp.float32)
    scaled = hidden32 * lax.rsqrt(jnp.mean(hidden32 * hidden32, -1, keepdims=True) + 1e-06)
    layer_input = (scaled * gain32).astype(jnp.bfloat16)
    queries = (
        jnp.einsum("btd,de->bte", layer_input, query_w, preferred_element_type=jnp.float32)
        * HD ** (-0.5)
    ).astype(jnp.bfloat16)
    key_t = jnp.einsum(
        "btd,de->bet", layer_input, key_w, preferred_element_type=jnp.float32
    ).astype(jnp.bfloat16)
    value_t = jnp.einsum(
        "btd,de->bet", layer_input, value_w, preferred_element_type=jnp.float32
    ).astype(jnp.bfloat16)
    kv_local = key_w.shape[1] // HD
    group_size = query_w.shape[1] // key_w.shape[1]
    key_t = key_t.reshape(batch_count, kv_local, HD, tok_count)
    value_t = value_t.reshape(batch_count, kv_local, HD, tok_count)
    query_rows = queries.reshape(batch_count, tok_count, kv_local, group_size, HD)
    query_pos = tok_start + jnp.arange(tok_count, dtype=jnp.int32)
    first_valid = total_tokens - seq_lens // STRIDE
    start_state = (
        jnp.full((batch_count, kv_local, group_size, tok_count), -1e30, jnp.float32),
        jnp.zeros((batch_count, kv_local, group_size, tok_count), jnp.float32),
        jnp.zeros((batch_count, kv_local, group_size, tok_count, HD), jnp.float32),
    )
    key_piece = lax.all_gather(key_t, "tm", axis=3, tiled=True)
    value_piece = lax.all_gather(value_t, "tm", axis=3, tiled=True)
    key_count = key_piece.shape[3]
    block_width = 1024 if key_count % 1024 == 0 else key_count
    rounds = key_count // block_width
    key_blocks = jnp.moveaxis(
        key_piece.reshape(batch_count, kv_local, HD, rounds, block_width), 3, 0
    )
    value_blocks = jnp.moveaxis(
        value_piece.reshape(batch_count, kv_local, HD, rounds, block_width), 3, 0
    )
    offsets = jnp.arange(rounds, dtype=jnp.int32) * block_width

    def scan_step(state, block_item):
        key_block, value_block, offset = block_item
        return (
            absorb_block(state, key_block, value_block, offset, query_rows, query_pos, first_valid),
            None,
        )

    result, _ = lax.scan(scan_step, start_state, (key_blocks, value_blocks, offsets))
    run_max, run_sum, accumulated = result
    attended = (accumulated / run_sum[..., None]).astype(jnp.bfloat16)
    attended = attended.transpose(0, 3, 1, 2, 4).reshape(
        batch_count, tok_count, kv_local * group_size * HD
    )
    partial_value = jnp.einsum("bte,ed->btd", attended, out_w, preferred_element_type=jnp.float32)
    head_total = lax.psum(partial_value.astype(jnp.bfloat16), "mp").astype(jnp.float32)
    new_hidden = (hidden32 + head_total).astype(jnp.bfloat16)
    return (new_hidden, key_t, value_t)


def per_device(
    series, lengths, patch_weight, norm_gain, query_weight, key_weight, value_weight, out_weight
):
    seq_count, channels, steps_dev = series.shape
    tok_count = steps_dev // STRIDE
    time_count = lax.axis_size("tm")
    time_at = lax.axis_index("tm")
    total_tokens = tok_count * time_count
    tok_start = time_at * tok_count
    step_pos = time_at * steps_dev + jnp.arange(steps_dev, dtype=jnp.int32)
    valid_steps = (step_pos[None, :] >= (steps_dev * time_count - lengths)[:, None]).astype(
        jnp.float32
    )
    masked = series.astype(jnp.float32) * valid_steps[:, None, :]
    history = lengths.astype(jnp.float32)[:, None]
    channel_total = lax.psum(jnp.sum(masked, -1), "tm")
    channel_mean = channel_total / history
    centered = (masked - channel_mean[..., None]) * valid_steps[:, None, :]
    spread_total = lax.psum(jnp.sum(centered * centered, -1), "tm")
    variance = spread_total / history
    normed = (centered * lax.rsqrt(variance + 1e-05)[..., None]).astype(jnp.bfloat16)
    blocks = normed.reshape(seq_count, channels, tok_count, STRIDE)
    column_count = patch_weight.shape[1]
    halves = patch_weight.reshape(channels, 2, STRIDE, column_count)
    right_terms = jnp.einsum(
        "scjr,crd->sjd", blocks, halves[:, 1], preferred_element_type=jnp.float32
    )
    left_all = jnp.einsum("scjr,crd->sjd", blocks, halves[:, 0], preferred_element_type=jnp.float32)
    prior_steps = from_behind(blocks[:, :, tok_count - 1, :], "tm", 1)
    edge_term = jnp.einsum(
        "scr,crd->sd", prior_steps, halves[:, 0], preferred_element_type=jnp.float32
    )
    left_terms = jnp.concatenate([edge_term[:, None, :], left_all[:, : tok_count - 1, :]], 1)
    tokens = (left_terms + right_terms).astype(jnp.bfloat16)
    gathered = lax.all_gather(tokens, ("mp", "section"), axis=2, tiled=True)
    feature_count = gathered.shape[2]
    section_count = lax.axis_size("section")
    section_at = lax.axis_index("section")
    per_section = seq_count // section_count
    head_cols = feature_count // lax.axis_size("mp")
    col_at = lax.axis_index("mp") * head_cols
    kv_local = key_weight.shape[2] // HD
    zero_index = jnp.int32(0)
    key_store = jnp.zeros((1, seq_count, kv_local, HD, tok_count), jnp.bfloat16)
    value_store = jnp.zeros((1, seq_count, kv_local, HD, tok_count), jnp.bfloat16)
    final_store = jnp.zeros((seq_count, tok_count, head_cols), jnp.bfloat16)
    incoming = jnp.zeros((1, tok_count, feature_count), jnp.bfloat16)
    tick_count = seq_count + section_count - 1
    for tick_index in range(tick_count):
        own_rows = gathered[min(tick_index, seq_count - 1)][None]
        current = jnp.where(section_at == 0, own_rows, incoming)
        seq_here = tick_index - section_at
        is_live = (seq_here >= 0) & (seq_here < seq_count)
        seq_slot = jnp.clip(seq_here, 0, seq_count - 1)
        seq_len = lax.dynamic_slice_in_dim(lengths, seq_slot, 1)
        result, key_t, value_t = attend_layer(
            current,
            seq_len,
            norm_gain[0],
            query_weight[0],
            key_weight[0],
            value_weight[0],
            out_weight[0],
            tok_start,
            total_tokens,
        )
        place = (zero_index, seq_slot, zero_index, zero_index, zero_index)
        key_store = jnp.where(
            is_live, lax.dynamic_update_slice(key_store, key_t[None], place), key_store
        )
        value_store = jnp.where(
            is_live, lax.dynamic_update_slice(value_store, value_t[None], place), value_store
        )
        columns = lax.dynamic_slice_in_dim(result, col_at, head_cols, 2)
        is_last = is_live & (section_at == section_count - 1)
        final_store = jnp.where(
            is_last,
            lax.dynamic_update_slice(final_store, columns, (seq_slot, zero_index, zero_index)),
            final_store,
        )
        if tick_index + 1 < tick_count:
            incoming = from_behind(result, "section", 1)
    broadcast_rows = from_root(final_store, "section", section_count - 1)
    final_cols = lax.dynamic_slice_in_dim(broadcast_rows, section_at * per_section, per_section, 0)
    return (key_store, value_store, final_cols)


def solution(mesh):
    in_specs = (
        P("groups", None, "tm"),
        P("groups"),
        P(None, ("mp", "section")),
        P("section", None),
        P("section", None, "mp"),
        P("section", None, "mp"),
        P("section", None, "mp"),
        P("section", "mp", None),
    )
    out_specs = (
        P("section", "groups", "mp", None, "tm"),
        P("section", "groups", "mp", None, "tm"),
        P(("groups", "section"), "tm", "mp"),
    )
    return jax.shard_map(
        per_device, mesh=mesh, in_specs=in_specs, out_specs=out_specs, check_vma=False
    )
```

profile of v0, /device:TPU:0, one launch (start us, length us, event | category | flops | bytes accessed | tf_op | source)
XLA Modules:
  0.0 291.1 jit_solution(578777108349074487)
XLA Ops:
  9.7 13.4 %psum.42 = f32[2,64]{1,0:T(2,128)S(1)} all-reduce(f32[2,64]{1,0:T(2,128)S(1)} %fusion.3), channel_id=1, replica_groups=mesh['groups'=2,'tm'=4,'mp'=2,'section'=2] {'tm'}, use_global_device_ids=true, to_apply=%region_1.0 | all-reduce | flops 128 | bytes 1024 | tf_op jit(solution)/shard_map/psum | solution.py:122
  23.2 1.8 multiply_reduce_fusion
  25.0 8.3 %psum.43 = f32[2,64]{1,0:T(2,128)S(1)} all-reduce(f32[2,64]{1,0:T(2,128)S(1)} %multiply_reduce_fusion), channel_id=1, replica_groups=mesh['groups'=2,'tm'=4,'mp'=2,'section'=2] {'tm'}, use_global_device_ids=true, to_apply=%region_3.0 | all-reduce | flops 128 | bytes 1024 | tf_op jit(solution)/shard_map/psum | solution.py:125
  34.8 5.6 %copy.25 = bf16[2,64,4096]{1,0,2:T(2,128)(2,1)} copy(bf16[2,64,4096]{2,1,0:T(8,128)(2,1)} %multiply_convert_fusion) | data formatting | bytes 2097152 | tf_op jit(solution)/shard_map/convert_element_type | solution.py:127
  41.1 3.9 %collective-permute-start = (bf16[2,64,32]{1,0,2:T(2,128)(2,1)S(1)}, bf16[2,64,32]{1,0,2:T(2,128)(2,1)S(1)}, u32[]{:S(2)}, u32[]{:S(2)}) collective-permute-start(bf16[2,64,32]{1,0,2:T(2,128)(2,1)S(1)} %slice_bitcast_fusion), channel_id=1, source_target_pairs={{0,4},{4,8},{8,12},{1,5},{5,9},{9,13},{2,6},{6,10},{10,14},{3,7},{... | collective-permute-start | bytes 24584 | tf_op jit(solution)/shard_map/ppermute | solution.py:13
  53.4 5.5 %copy.28 = bf16[2,64,128,32]{2,1,3,0:T(8,128)(2,1)} copy(bf16[2,64,128,32]{1,0,3,2:T(2,128)(2,1)} %bitcast.265) | data formatting | bytes 2097152 | tf_op jit(solution)/shard_map/reshape | solution.py:128
  58.9 4.5 %copy.26 = bf16[4096,320]{1,0:T(8,128)(2,1)} copy(bf16[4096,320]{0,1:T(8,128)(2,1)} %param.10) | data formatting | bytes 5242880 | tf_op args[2]
  63.4 2.3 fusion.128
  69.4 2.0 fusion.59
  72.4 2.2 fusion.46
  74.6 8.0 %all_gather.21 = bf16[2,128,1280]{1,2,0:T(8,128)(2,1)S(1)} all-gather(bf16[2,128,320]{1,2,0:T(8,128)(2,1)S(1)} %fusion.46), channel_id=1, replica_groups=mesh['groups'=2,'tm'=4,'mp'=2,'section'=2] {'mp','section'}, dimensions={2}, use_global_device_ids=true | all-gather | bytes 819200 | tf_op jit(solution)/shard_map/all_gather | solution.py:141
  85.0 13.2 %all_gather.23 = bf16[1,2,80,512]{3,2,1,0:T(8,128)(2,1)} all-gather(bf16[1,2,80,128]{3,2,1,0:T(8,128)(2,1)S(1)} %bitcast.283), channel_id=1, replica_groups=mesh['groups'=2,'tm'=4,'mp'=2,'section'=2] {'tm'}, dimensions={3}, use_global_device_ids=true | all-gather | bytes 204800 | tf_op jit(solution)/shard_map/all_gather | solution.py:76
  98.2 12.4 %all_gather.22 = bf16[1,2,80,512]{3,2,1,0:T(8,128)(2,1)S(1)} all-gather(bf16[1,2,80,128]{3,2,1,0:T(8,128)(2,1)S(1)} %bitcast.282), channel_id=1, replica_groups=mesh['groups'=2,'tm'=4,'mp'=2,'section'=2] {'tm'}, dimensions={3}, use_global_device_ids=true | all-gather | bytes 204800 | tf_op jit(solution)/shard_map/all_gather | solution.py:75
  117.6 22.0 %all-reduce.5.cloned.1.call-done = bf16[1,128,1280]{1,2,0:T(8,128)(2,1)} async-done(((bf16[1,128,1280]{1,2,0:T(8,128)(2,1)}), bf16[1,128,1280]{1,2,0:T(8,128)(2,1)}) %all-reduce.5.cloned.1.call-update) | async-done | bytes 327696 | tf_op jit(solution)/shard_map/psum | solution.py:102
  140.8 1.7 collective-permute-start.1
  148.3 12.4 %all_gather.24 = bf16[1,2,80,512]{3,2,1,0:T(8,128)(2,1)S(1)} all-gather(bf16[1,2,80,128]{3,2,1,0:T(8,128)(2,1)S(1)} %bitcast.274), channel_id=1, replica_groups=mesh['groups'=2,'tm'=4,'mp'=2,'section'=2] {'tm'}, dimensions={3}, use_global_device_ids=true | all-gather | bytes 204800 | tf_op jit(solution)/shard_map/all_gather | solution.py:75
  162.5 12.7 %all_gather.25 = bf16[1,2,80,512]{3,2,1,0:T(8,128)(2,1)S(1)} all-gather(bf16[1,2,80,128]{3,2,1,0:T(8,128)(2,1)S(1)} %bitcast.272), channel_id=1, replica_groups=mesh['groups'=2,'tm'=4,'mp'=2,'section'=2] {'tm'}, dimensions={3}, use_global_device_ids=true | all-gather | bytes 204800 | tf_op jit(solution)/shard_map/all_gather | solution.py:76
  180.7 20.6 %all-reduce.7.cloned.1.call-done = bf16[1,128,1280]{1,2,0:T(8,128)(2,1)} async-done(((bf16[1,128,1280]{1,2,0:T(8,128)(2,1)}), bf16[1,128,1280]{1,2,0:T(8,128)(2,1)}) %all-reduce.7.cloned.1.call-update) | async-done | bytes 327696 | tf_op jit(solution)/shard_map/psum | solution.py:102
  202.6 1.9 collective-permute-start.2
  206.4 1.9 fusion.127
  211.5 12.6 %all_gather.27 = bf16[1,2,80,512]{3,2,1,0:T(8,128)(2,1)S(1)} all-gather(bf16[1,2,80,128]{3,2,1,0:T(8,128)(2,1)} %bitcast.276), channel_id=1, replica_groups=mesh['groups'=2,'tm'=4,'mp'=2,'section'=2] {'tm'}, dimensions={3}, use_global_device_ids=true | all-gather | bytes 204800 | tf_op jit(solution)/shard_map/all_gather | solution.py:76
  224.1 12.6 %all_gather.26 = bf16[1,2,80,512]{3,2,1,0:T(8,128)(2,1)S(1)} all-gather(bf16[1,2,80,128]{3,2,1,0:T(8,128)(2,1)} %bitcast.278), channel_id=1, replica_groups=mesh['groups'=2,'tm'=4,'mp'=2,'section'=2] {'tm'}, dimensions={3}, use_global_device_ids=true | all-gather | bytes 204800 | tf_op jit(solution)/shard_map/all_gather | solution.py:75
  239.9 22.2 %all-reduce.9.cloned.1.call-done = bf16[1,128,1280]{1,2,0:T(8,128)(2,1)} async-done(((bf16[1,128,1280]{1,2,0:T(8,128)(2,1)}), bf16[1,128,1280]{1,2,0:T(8,128)(2,1)}) %all-reduce.9.cloned.1.call-update) | async-done | bytes 327696 | tf_op jit(solution)/shard_map/psum | solution.py:102
  264.0 18.8 %all-reduce.11.cloned.1.call-done = bf16[2,128,640]{1,2,0:T(8,128)(2,1)} async-done(((bf16[2,128,640]{1,2,0:T(8,128)(2,1)}), bf16[2,128,640]{1,2,0:T(8,128)(2,1)}) %all-reduce.11.cloned.1.call-update) | async-done | bytes 327696 | tf_op jit(solution)/shard_map/psum | solution.py:18
  (144 shorter events, 46.4 us)
Async XLA Ops:
  7.2 108.9 %copy-start = (bf16[1,640,1280]{2,1,0:T(8,128)(2,1)S(1)}, bf16[1,640,1280]{2,1,0:T(8,128)(2,1)}, u32[]{:S(2)}) copy-start(bf16[1,640,1280]{2,1,0:T(8,128)(2,1)} %param.15) | copy-start | bytes 4915204
  7.2 26.2 %copy-start.1 = (bf16[2,64,4096]{2,1,0:T(8,128)(2,1)S(1)}, bf16[2,64,4096]{2,1,0:T(8,128)(2,1)}, u32[]{:S(2)}) copy-start(bf16[2,64,4096]{2,1,0:T(8,128)(2,1)} %param.8) | copy-start | bytes 3145732
  7.2 132.4 %all-reduce.5.cloned.1.call-start = ((), (), s32[]{:S(2)}) async-start(), calls=%async_computation | async-start | bytes 655360 | tf_op jit(solution)/shard_map/psum | solution.py:102
  34.8 10.2 %copy-start.26 = (s32[2]{0:T(128)S(1)}, s32[2]{0:T(128)}, u32[]{:S(2)}) copy-start(s32[2]{0:T(128)} %param.9) | copy-start | bytes 28
  41.1 28.3 %collective-permute-start = (bf16[2,64,32]{1,0,2:T(2,128)(2,1)S(1)}, bf16[2,64,32]{1,0,2:T(2,128)(2,1)S(1)}, u32[]{:S(2)}, u32[]{:S(2)}) collective-permute-start(bf16[2,64,32]{1,0,2:T(2,128)(2,1)S(1)} %slice_bitcast_fusion), channel_id=1, source_target_pairs={{0,4},{4,8},{8,12},{1,5},{5,9},{9,13},{2,6},{6,10},{10,14},{3,7},{... | collective-permute-start | bytes 24584 | tf_op jit(solution)/shard_map/ppermute | solution.py:13
  72.4 10.5 %copy-start.27 = (bf16[1,1280,160]{1,2,0:T(8,128)(2,1)S(1)}, bf16[1,1280,160]{1,2,0:T(8,128)(2,1)}, u32[]{:S(2)}) copy-start(bf16[1,1280,160]{1,2,0:T(8,128)(2,1)} %param.13) | copy-start | bytes 1228804
  74.6 9.3 %copy-start.29 = (bf16[1,1280,160]{1,2,0:T(8,128)(2,1)S(1)}, bf16[1,1280,160]{1,2,0:T(8,128)(2,1)}, u32[]{:S(2)}) copy-start(bf16[1,1280,160]{1,2,0:T(8,128)(2,1)} %param.14) | copy-start | bytes 1228804
  74.6 35.9 %copy-start.2 = (bf16[1,1280,640]{2,1,0:T(8,128)(2,1)S(1)}, bf16[1,1280,640]{2,1,0:T(8,128)(2,1)}, u32[]{:S(2)}) copy-start(bf16[1,1280,640]{2,1,0:T(8,128)(2,1)} %param.12) | copy-start | bytes 4915204
  82.7 27.9 %copy-start.3 = (bf16[2,128,1280]{1,2,0:T(8,128)(2,1)}, bf16[2,128,1280]{1,2,0:T(8,128)(2,1)S(1)}, u32[]{:S(2)}) copy-start(bf16[2,128,1280]{1,2,0:T(8,128)(2,1)S(1)} %all_gather.21) | copy-start | bytes 1966084
  117.6 83.8 %all-reduce.7.cloned.1.call-start = ((), (), s32[]{:S(2)}) async-start(), calls=%async_computation.1 | async-start | bytes 655360 | tf_op jit(solution)/shard_map/psum | solution.py:102
  140.8 3.0 %collective-permute-start.1 = (bf16[1,128,1280]{1,2,0:T(8,128)(2,1)S(1)}, bf16[1,128,1280]{1,2,0:T(8,128)(2,1)S(1)}, u32[]{:S(2)}, u32[]{:S(2)}) collective-permute-start(bf16[1,128,1280]{1,2,0:T(8,128)(2,1)S(1)} %fusion.80), channel_id=1, source_target_pairs={{0,1},{2,3},{4,5},{6,7},{8,9},{10,11},{12,13},{14,15},{16,17},{18,... | collective-permute-start | bytes 983048 | tf_op jit(solution)/shard_map/ppermute | solution.py:13
  162.5 14.1 %copy-start.13 = (pred[128,512]{0,1:T(8,128)(4,1)S(1)}, pred[128,512]{0,1:T(8,128)(4,1)}, u32[]{:S(2)}) copy-start(pred[128,512]{0,1:T(8,128)(4,1)} %get-tuple-element.94) | copy-start | bytes 196612
  179.0 83.1 %all-reduce.9.cloned.1.call-start = ((), (), s32[]{:S(2)}) async-start(), calls=%async_computation.2 | async-start | bytes 655360 | tf_op jit(solution)/shard_map/psum | solution.py:102
  180.7 28.8 %copy-start.18 = (bf16[1,2,2,80,128]{4,3,2,1,0:T(8,128)(2,1)}, bf16[1,2,2,80,128]{4,3,2,1,0:T(8,128)(2,1)S(1)}, u32[]{:S(2)}) copy-start(bf16[1,2,2,80,128]{4,3,2,1,0:T(8,128)(2,1)S(1)} %constant_dynamic-update-slice_fusion) | copy-start | bytes 245764
  201.3 7.2 %copy-start.28 = (bf16[1,1280,160]{1,2,0:T(8,128)(2,1)S(1)}, bf16[1,1280,160]{1,2,0:T(8,128)(2,1)}, u32[]{:S(2)}) copy-start(bf16[1,1280,160]{1,2,0:T(8,128)(2,1)} %param.13) | copy-start | bytes 1228804
  202.6 7.0 %copy-start.31 = (bf16[1,1280,160]{1,2,0:T(8,128)(2,1)S(1)}, bf16[1,1280,160]{1,2,0:T(8,128)(2,1)}, u32[]{:S(2)}) copy-start(bf16[1,1280,160]{1,2,0:T(8,128)(2,1)} %param.14) | copy-start | bytes 1228804
  202.6 3.8 %collective-permute-start.2 = (bf16[1,128,1280]{1,2,0:T(8,128)(2,1)S(1)}, bf16[1,128,1280]{1,2,0:T(8,128)(2,1)S(1)}, u32[]{:S(2)}, u32[]{:S(2)}) collective-permute-start(bf16[1,128,1280]{1,2,0:T(8,128)(2,1)S(1)} %fusion.84), channel_id=1, source_target_pairs={{0,1},{2,3},{4,5},{6,7},{8,9},{10,11},{12,13},{14,15},{16,17},{18,... | collective-permute-start | bytes 983048 | tf_op jit(solution)/shard_map/ppermute | solution.py:13
  238.2 23.9 %copy-start.8 = (f32[1,128,1280]{1,2,0:T(8,128)S(1)}, f32[1,128,1280]{1,2,0:T(8,128)}, u32[]{:S(2)}) copy-start(f32[1,128,1280]{1,2,0:T(8,128)} %get-tuple-element.72) | copy-start | bytes 1966084
  238.2 25.7 %copy-start.16 = (bf16[1,2,2,80,128]{4,3,2,1,0:T(8,128)(2,1)S(1)}, bf16[1,2,2,80,128]{4,3,2,1,0:T(8,128)(2,1)}, u32[]{:S(2)}) copy-start(bf16[1,2,2,80,128]{4,3,2,1,0:T(8,128)(2,1)} %copy-done.15) | copy-start | bytes 245764
  238.2 25.7 %copy-start.24 = (bf16[128,160]{0,1:T(8,128)(2,1)S(1)}, bf16[128,160]{0,1:T(8,128)(2,1)}, u32[]{:S(2)}) copy-start(bf16[128,160]{0,1:T(8,128)(2,1)} %convolution_convert_fusion.4) | copy-start | bytes 122884
  238.2 25.7 %copy-start.23 = (bf16[128,160]{0,1:T(8,128)(2,1)S(1)}, bf16[128,160]{0,1:T(8,128)(2,1)}, u32[]{:S(2)}) copy-start(bf16[128,160]{0,1:T(8,128)(2,1)} %convolution_convert_fusion.3) | copy-start | bytes 122884
  239.7 43.1 %all-reduce.11.cloned.1.call-start = ((), (), s32[]{:S(2)}) async-start(), calls=%async_computation.3 | async-start | bytes 655360 | tf_op jit(solution)/shard_map/psum | solution.py:18
  263.9 20.6 %copy-start.17 = (bf16[1,2,2,80,128]{4,3,2,1,0:T(8,128)(2,1)}, bf16[1,2,2,80,128]{4,3,2,1,0:T(8,128)(2,1)S(1)}, u32[]{:S(2)}) copy-start(bf16[1,2,2,80,128]{4,3,2,1,0:T(8,128)(2,1)S(1)} %select_dynamic-update-slice_fusion.4) | copy-start | bytes 245764
  264.0 20.6 %copy-start.20 = (bf16[1,2,2,80,128]{4,3,2,1,0:T(8,128)(2,1)}, bf16[1,2,2,80,128]{4,3,2,1,0:T(8,128)(2,1)S(1)}, u32[]{:S(2)}) copy-start(bf16[1,2,2,80,128]{4,3,2,1,0:T(8,128)(2,1)S(1)} %select_dynamic-update-slice_fusion.2) | copy-start | bytes 245764
  (15 other events, 36.9 us)
Sparse Core Ops, SparseCore 0:
  117.7 21.8 all-reduce.4
  179.2 22.1 all-reduce.6
  239.8 22.2 all-reduce.8
  264.4 18.3 all-reduce.10
where the time goes:
time: 293 us; the launch traced here: 291 us
  blocking collectives  106 us (36%)
  waiting for transfers between devices  84.9 us (29%)
  local copies, waits for them, and re-layouts  28.5 us (10%)
  matrix products  24.7 us (8%)
  between operations  22.1 us (8%)
  other arithmetic  17.6 us (6%)
  starting transfers between devices  7.62 us (3%)
    psum x3, waiting for transfers between devices, attend_layer(): lax.psum(partial_value.astype(jnp.bfloat16), 'mp').astype(jnp.float32)  64.8 us
    all_gather x3, blocking collectives, attend_layer(): value_piece = lax.all_gather(value_t, 'tm', axis=3, tiled=True)  38.5 us
    all_gather x3, blocking collectives, attend_layer(): key_piece = lax.all_gather(key_t, 'tm', axis=3, tiled=True)  37.4 us
    psum x1, waiting for transfers between devices, from_root(): return lax.psum(jnp.where(mine, value, jnp.zeros_like(value)), axis)  18.8 us
    psum x1, blocking collectives, per_device(): channel_total = lax.psum(jnp.sum(masked, -1), 'tm')  13.4 us
    psum x1, blocking collectives, per_device(): spread_total = lax.psum(jnp.sum(centered * centered, -1), 'tm')  8.34 us
    all_gather x1, blocking collectives, per_device(): gathered = lax.all_gather(tokens, ('mp', 'section'), axis=2, tiled=True)  8.02 us
    ppermute x3, starting transfers between devices, from_behind(): return lax.ppermute(value, axis, pairs)  7.46 us
  transfers between devices with their start and end apart: 7, of which 5 were waited for; matrix products, arithmetic and copies ran while one was open for 7% of the time, Pallas kernels for 0%

commit v1 on v0

--- a/solution.py
+++ b/solution.py
@@ -99,7 +99,9 @@
         batch_count, tok_count, kv_local * group_size * HD
     )
     partial_value = jnp.einsum("bte,ed->btd", attended, out_w, preferred_element_type=jnp.float32)
-    head_total = lax.psum(partial_value.astype(jnp.bfloat16), "mp").astype(jnp.float32)
+    head_total = jnp.sum(lax.all_gather(partial_value.astype(jnp.bfloat16), "mp"), axis=0).astype(
+        jnp.float32
+    )
     new_hidden = (hidden32 + head_total).astype(jnp.bfloat16)
     return (new_hidden, key_t, value_t)
 

time: 293 us -> 250 us (0.85)
  waiting for transfers between devices: 84.9 us -> 16.3 us
  blocking collectives: 106 us -> 130 us
  matrix products: 24.7 us -> 19.3 us
  local copies, waits for them, and re-layouts: 28.5 us -> 32.6 us
  other arithmetic: 17.6 us -> 21.3 us
    psum x3 -> x0, waiting for transfers between devices: 64.8 us -> none  [attend_layer(): lax.psum(partial_value.astype(jnp.bfloat16), 'mp').astype(jnp.float32)]
    all_gather x0 -> x3, blocking collectives: none -> 23.7 us  [attend_layer(): lax.all_gather(partial_value.astype(jnp.bfloat16), 'mp')]
    reduce_sum x0 -> x3, local copies, waits for them, and re-layouts: none -> 4.95 us  [attend_layer(): jnp.sum(lax.all_gather(partial_value.astype(jnp.bfloat16), 'mp'), axis=0)]
    reduce_sum x0 -> x3, other arithmetic: none -> 4.93 us  [attend_layer(): jnp.sum(lax.all_gather(partial_value.astype(jnp.bfloat16), 'mp'), axis=0)]
    dot_general x3, matrix products: 4.4 us -> 1.36 us  [attend_layer(): jnp.einsum('bte,ed->btd', attended, out_w, preferred_element_type=jnp.flo...]
    unnamed x66 -> x72, local copies, waits for them, and re-layouts: 6.62 us -> 7.4 us
  transfers between devices with their start and end apart: 7 -> 4, of which waited for: 5 -> 2; matrix products, arithmetic and copies ran while one was open for 7% -> 7% of each run, Pallas kernels for 0% -> 0%
where the time goes in v1:
time: 250 us; the launch traced here: 248 us
  blocking collectives  130 us (52%)
  local copies, waits for them, and re-layouts  32.6 us (13%)
  between operations  22.4 us (9%)
  other arithmetic  21.3 us (9%)
  matrix products  19.3 us (8%)
  waiting for transfers between devices  16.3 us (7%)
  starting transfers between devices  6.53 us (3%)
    all_gather x3, blocking collectives, attend_layer(): value_piece = lax.all_gather(value_t, 'tm', axis=3, tiled=True)  38.3 us
    all_gather x3, blocking collectives, attend_layer(): key_piece = lax.all_gather(key_t, 'tm', axis=3, tiled=True)  37.8 us
    all_gather x3, blocking collectives, attend_layer(): lax.all_gather(partial_value.astype(jnp.bfloat16), 'mp')  23.7 us
    psum x1, waiting for transfers between devices, from_root(): return lax.psum(jnp.where(mine, value, jnp.zeros_like(value)), axis)  16 us
    psum x1, blocking collectives, per_device(): channel_total = lax.psum(jnp.sum(masked, -1), 'tm')  13.4 us
    psum x1, blocking collectives, per_device(): spread_total = lax.psum(jnp.sum(centered * centered, -1), 'tm')  8.34 us
    all_gather x1, blocking collectives, per_device(): gathered = lax.all_gather(tokens, ('mp', 'section'), axis=2, tiled=True)  8.02 us
    unnamed x72, local copies, waits for them, and re-layouts  7.4 us
  transfers between devices with their start and end apart: 4, of which 2 were waited for; matrix products, arithmetic and copies ran while one was open for 7% of the time, Pallas kernels for 0%

profile of v1, /device:TPU:0, one launch (start us, length us, event | category | flops | bytes accessed | tf_op | source)
XLA Modules:
  0.0 248.1 jit_solution(220440323562897756)
XLA Ops:
  9.7 13.4 %psum.21 = f32[2,64]{1,0:T(2,128)S(1)} all-reduce(f32[2,64]{1,0:T(2,128)S(1)} %fusion), channel_id=1, replica_groups=mesh['groups'=2,'tm'=4,'mp'=2,'section'=2] {'tm'}, use_global_device_ids=true, to_apply=%region_1.0 | all-reduce | flops 128 | bytes 1024 | tf_op jit(solution)/shard_map/psum | solution.py:124
  25.0 8.3 %psum.22 = f32[2,64]{1,0:T(2,128)S(1)} all-reduce(f32[2,64]{1,0:T(2,128)S(1)} %multiply_reduce_fusion), channel_id=1, replica_groups=mesh['groups'=2,'tm'=4,'mp'=2,'section'=2] {'tm'}, use_global_device_ids=true, to_apply=%region_3.0 | all-reduce | flops 128 | bytes 1024 | tf_op jit(solution)/shard_map/psum | solution.py:127
  34.8 5.5 %copy.36 = bf16[2,64,4096]{1,0,2:T(2,128)(2,1)} copy(bf16[2,64,4096]{2,1,0:T(8,128)(2,1)} %multiply_convert_fusion) | data formatting | bytes 2097152 | tf_op jit(solution)/shard_map/convert_element_type | solution.py:129
  41.1 3.9 %collective-permute-start = (bf16[2,64,32]{1,0,2:T(2,128)(2,1)S(1)}, bf16[2,64,32]{1,0,2:T(2,128)(2,1)S(1)}, u32[]{:S(2)}, u32[]{:S(2)}) collective-permute-start(bf16[2,64,32]{1,0,2:T(2,128)(2,1)S(1)} %slice_bitcast_fusion), channel_id=1, source_target_pairs={{0,4},{4,8},{8,12},{1,5},{5,9},{9,13},{2,6},{6,10},{10,14},{3,7},{... | collective-permute-start | bytes 24584 | tf_op jit(solution)/shard_map/ppermute | solution.py:13
  53.4 5.5 %copy.39 = bf16[2,64,128,32]{2,1,3,0:T(8,128)(2,1)} copy(bf16[2,64,128,32]{1,0,3,2:T(2,128)(2,1)} %bitcast.270) | data formatting | bytes 2097152 | tf_op jit(solution)/shard_map/reshape | solution.py:130
  58.9 4.6 %copy.37 = bf16[4096,320]{1,0:T(8,128)(2,1)} copy(bf16[4096,320]{0,1:T(8,128)(2,1)} %param.10) | data formatting | bytes 5242880 | tf_op args[2]
  63.5 2.3 fusion.125
  69.5 2.0 fusion.56
  72.4 2.2 fusion.43
  74.7 8.0 %all_gather.39 = bf16[2,128,1280]{1,2,0:T(8,128)(2,1)S(1)} all-gather(bf16[2,128,320]{1,2,0:T(8,128)(2,1)S(1)} %fusion.43), channel_id=1, replica_groups=mesh['groups'=2,'tm'=4,'mp'=2,'section'=2] {'mp','section'}, dimensions={2}, use_global_device_ids=true | all-gather | bytes 819200 | tf_op jit(solution)/shard_map/all_gather | solution.py:143
  84.4 13.2 %all_gather.41 = bf16[1,2,80,512]{3,2,1,0:T(8,128)(2,1)} all-gather(bf16[1,2,80,128]{3,2,1,0:T(8,128)(2,1)S(1)} %bitcast.292), channel_id=1, replica_groups=mesh['groups'=2,'tm'=4,'mp'=2,'section'=2] {'tm'}, dimensions={3}, use_global_device_ids=true | all-gather | bytes 204800 | tf_op jit(solution)/shard_map/all_gather | solution.py:76
  97.6 12.4 %all_gather.40 = bf16[1,2,80,512]{3,2,1,0:T(8,128)(2,1)S(1)} all-gather(bf16[1,2,80,128]{3,2,1,0:T(8,128)(2,1)S(1)} %bitcast.291), channel_id=1, replica_groups=mesh['groups'=2,'tm'=4,'mp'=2,'section'=2] {'tm'}, dimensions={3}, use_global_device_ids=true | all-gather | bytes 204800 | tf_op jit(solution)/shard_map/all_gather | solution.py:75
  116.0 7.9 %all-gather = bf16[256,1280]{1,0:T(8,128)(2,1)} all-gather(bf16[128,1280]{1,0:T(8,128)(2,1)S(1)} %convolution_convert_fusion.2), channel_id=2, replica_groups=mesh['groups'=2,'tm'=4,'mp'=2,'section'=2] {'mp'}, dimensions={0}, use_global_device_ids=true | all-gather | bytes 983040 | tf_op jit(solution)/shard_map/all_gather | solution.py:102
  123.8 2.0 reduce.15
  125.8 1.9 copy.45
  134.0 12.7 %all_gather.44 = bf16[1,2,80,512]{3,2,1,0:T(8,128)(2,1)S(1)} all-gather(bf16[1,2,80,128]{3,2,1,0:T(8,128)(2,1)S(1)} %bitcast.287), channel_id=1, replica_groups=mesh['groups'=2,'tm'=4,'mp'=2,'section'=2] {'tm'}, dimensions={3}, use_global_device_ids=true | all-gather | bytes 204800 | tf_op jit(solution)/shard_map/all_gather | solution.py:75
  148.4 12.7 %all_gather.45 = bf16[1,2,80,512]{3,2,1,0:T(8,128)(2,1)S(1)} all-gather(bf16[1,2,80,128]{3,2,1,0:T(8,128)(2,1)S(1)} %bitcast.285), channel_id=1, replica_groups=mesh['groups'=2,'tm'=4,'mp'=2,'section'=2] {'tm'}, dimensions={3}, use_global_device_ids=true | all-gather | bytes 204800 | tf_op jit(solution)/shard_map/all_gather | solution.py:76
  164.0 8.0 %all-gather.1 = bf16[256,1280]{1,0:T(8,128)(2,1)} all-gather(bf16[128,1280]{1,0:T(8,128)(2,1)S(1)} %convolution_convert_fusion.1), channel_id=3, replica_groups=mesh['groups'=2,'tm'=4,'mp'=2,'section'=2] {'mp'}, dimensions={0}, use_global_device_ids=true | all-gather | bytes 983040 | tf_op jit(solution)/shard_map/all_gather | solution.py:102
  172.0 2.0 reduce.16
  181.0 1.9 fusion.124
  185.4 12.4 %all_gather.49 = bf16[1,2,80,512]{3,2,1,0:T(8,128)(2,1)S(1)} all-gather(bf16[1,2,80,128]{3,2,1,0:T(8,128)(2,1)S(1)} %bitcast.281), channel_id=1, replica_groups=mesh['groups'=2,'tm'=4,'mp'=2,'section'=2] {'tm'}, dimensions={3}, use_global_device_ids=true | all-gather | bytes 204800 | tf_op jit(solution)/shard_map/all_gather | solution.py:76
  197.8 12.7 %all_gather.48 = bf16[1,2,80,512]{3,2,1,0:T(8,128)(2,1)S(1)} all-gather(bf16[1,2,80,128]{3,2,1,0:T(8,128)(2,1)} %bitcast.283), channel_id=1, replica_groups=mesh['groups'=2,'tm'=4,'mp'=2,'section'=2] {'tm'}, dimensions={3}, use_global_device_ids=true | all-gather | bytes 204800 | tf_op jit(solution)/shard_map/all_gather | solution.py:75
  212.5 7.9 %all-gather.2 = bf16[256,1280]{1,0:T(8,128)(2,1)S(1)} all-gather(bf16[128,1280]{1,0:T(8,128)(2,1)S(1)} %convolution_convert_fusion), channel_id=4, replica_groups=mesh['groups'=2,'tm'=4,'mp'=2,'section'=2] {'mp'}, dimensions={0}, use_global_device_ids=true | all-gather | bytes 983040 | tf_op jit(solution)/shard_map/all_gather | solution.py:102
  223.5 16.0 %all-reduce.2.cloned.1.call-done = bf16[2,128,640]{1,2,0:T(8,128)(2,1)} async-done(((bf16[2,128,640]{1,2,0:T(8,128)(2,1)}), bf16[2,128,640]{1,2,0:T(8,128)(2,1)}) %all-reduce.2.cloned.1.call-update) | async-done | bytes 327696 | tf_op jit(solution)/shard_map/psum | solution.py:18
  (150 shorter events, 46.2 us)
Async XLA Ops:
  7.2 108.3 %copy-start = (bf16[1,640,1280]{2,1,0:T(8,128)(2,1)S(1)}, bf16[1,640,1280]{2,1,0:T(8,128)(2,1)}, u32[]{:S(2)}) copy-start(bf16[1,640,1280]{2,1,0:T(8,128)(2,1)} %param.15) | copy-start | bytes 4915204
  7.2 26.2 %copy-start.1 = (bf16[2,64,4096]{2,1,0:T(8,128)(2,1)S(1)}, bf16[2,64,4096]{2,1,0:T(8,128)(2,1)}, u32[]{:S(2)}) copy-start(bf16[2,64,4096]{2,1,0:T(8,128)(2,1)} %param.8) | copy-start | bytes 3145732
  7.2 232.3 %all-reduce.2.cloned.1.call-start = ((), (), s32[]{:S(2)}) async-start(), calls=%async_computation | async-start | bytes 655360 | tf_op jit(solution)/shard_map/psum | solution.py:18
  34.8 10.2 %copy-start.28 = (s32[2]{0:T(128)S(1)}, s32[2]{0:T(128)}, u32[]{:S(2)}) copy-start(s32[2]{0:T(128)} %param.9) | copy-start | bytes 28
  41.1 28.4 %collective-permute-start = (bf16[2,64,32]{1,0,2:T(2,128)(2,1)S(1)}, bf16[2,64,32]{1,0,2:T(2,128)(2,1)S(1)}, u32[]{:S(2)}, u32[]{:S(2)}) collective-permute-start(bf16[2,64,32]{1,0,2:T(2,128)(2,1)S(1)} %slice_bitcast_fusion), channel_id=1, source_target_pairs={{0,4},{4,8},{8,12},{1,5},{5,9},{9,13},{2,6},{6,10},{10,14},{3,7},{... | collective-permute-start | bytes 24584 | tf_op jit(solution)/shard_map/ppermute | solution.py:13
  72.4 10.5 %copy-start.29 = (bf16[1,1280,160]{1,2,0:T(8,128)(2,1)S(1)}, bf16[1,1280,160]{1,2,0:T(8,128)(2,1)}, u32[]{:S(2)}) copy-start(bf16[1,1280,160]{1,2,0:T(8,128)(2,1)} %param.13) | copy-start | bytes 1228804
  74.6 9.3 %copy-start.32 = (bf16[1,1280,160]{1,2,0:T(8,128)(2,1)S(1)}, bf16[1,1280,160]{1,2,0:T(8,128)(2,1)}, u32[]{:S(2)}) copy-start(bf16[1,1280,160]{1,2,0:T(8,128)(2,1)} %param.14) | copy-start | bytes 1228804
  74.7 35.3 %copy-start.2 = (bf16[1,1280,640]{2,1,0:T(8,128)(2,1)S(1)}, bf16[1,1280,640]{2,1,0:T(8,128)(2,1)}, u32[]{:S(2)}) copy-start(bf16[1,1280,640]{2,1,0:T(8,128)(2,1)} %param.12) | copy-start | bytes 4915204
  82.7 27.3 %copy-start.3 = (bf16[2,128,1280]{1,2,0:T(8,128)(2,1)}, bf16[2,128,1280]{1,2,0:T(8,128)(2,1)S(1)}, u32[]{:S(2)}) copy-start(bf16[2,128,1280]{1,2,0:T(8,128)(2,1)S(1)} %all_gather.39) | copy-start | bytes 1966084
  115.9 14.4 %copy-start.26 = (bf16[160,128]{1,0:T(8,128)(2,1)S(1)}, bf16[160,128]{1,0:T(8,128)(2,1)}, u32[]{:S(2)}) copy-start(bf16[160,128]{1,0:T(8,128)(2,1)} %get-tuple-element.113) | copy-start | bytes 122884
  129.0 2.5 %collective-permute-start.1 = (bf16[1,128,1280]{1,2,0:T(8,128)(2,1)S(1)}, bf16[1,128,1280]{1,2,0:T(8,128)(2,1)S(1)}, u32[]{:S(2)}, u32[]{:S(2)}) collective-permute-start(bf16[1,128,1280]{1,2,0:T(8,128)(2,1)S(1)} %fusion.77), channel_id=1, source_target_pairs={{0,1},{2,3},{4,5},{6,7},{8,9},{10,11},{12,13},{14,15},{16,17},{18,... | collective-permute-start | bytes 983048 | tf_op jit(solution)/shard_map/ppermute | solution.py:13
  148.4 14.1 %copy-start.11 = (pred[128,512]{0,1:T(8,128)(4,1)S(1)}, pred[128,512]{0,1:T(8,128)(4,1)}, u32[]{:S(2)}) copy-start(pred[128,512]{0,1:T(8,128)(4,1)} %get-tuple-element.97) | copy-start | bytes 196612
  164.0 14.5 %copy-start.14 = (bf16[1,2,2,80,128]{4,3,2,1,0:T(8,128)(2,1)S(1)}, bf16[1,2,2,80,128]{4,3,2,1,0:T(8,128)(2,1)}, u32[]{:S(2)}) copy-start(bf16[1,2,2,80,128]{4,3,2,1,0:T(8,128)(2,1)} %copy-done.13) | copy-start | bytes 245764
  164.0 17.0 %copy-start.19 = (bf16[1,2,2,80,128]{4,3,2,1,0:T(8,128)(2,1)S(1)}, bf16[1,2,2,80,128]{4,3,2,1,0:T(8,128)(2,1)}, u32[]{:S(2)}) copy-start(bf16[1,2,2,80,128]{4,3,2,1,0:T(8,128)(2,1)} %copy-done.18) | copy-start | bytes 245764
  175.9 7.2 %copy-start.31 = (bf16[1,1280,160]{1,2,0:T(8,128)(2,1)S(1)}, bf16[1,1280,160]{1,2,0:T(8,128)(2,1)}, u32[]{:S(2)}) copy-start(bf16[1,1280,160]{1,2,0:T(8,128)(2,1)} %param.13) | copy-start | bytes 1228804
  175.9 8.3 %copy-start.34 = (bf16[1,1280,160]{1,2,0:T(8,128)(2,1)S(1)}, bf16[1,1280,160]{1,2,0:T(8,128)(2,1)}, u32[]{:S(2)}) copy-start(bf16[1,1280,160]{1,2,0:T(8,128)(2,1)} %param.14) | copy-start | bytes 1228804
  177.1 3.8 %collective-permute-start.2 = (bf16[1,128,1280]{1,2,0:T(8,128)(2,1)S(1)}, bf16[1,128,1280]{1,2,0:T(8,128)(2,1)S(1)}, u32[]{:S(2)}, u32[]{:S(2)}) collective-permute-start(bf16[1,128,1280]{1,2,0:T(8,128)(2,1)S(1)} %fusion.81), channel_id=1, source_target_pairs={{0,1},{2,3},{4,5},{6,7},{8,9},{10,11},{12,13},{14,15},{16,17},{18,... | collective-permute-start | bytes 983048 | tf_op jit(solution)/shard_map/ppermute | solution.py:13
  212.0 10.5 %copy-start.7 = (bf16[2,128,640]{1,2,0:T(8,128)(2,1)S(1)}, bf16[2,128,640]{1,2,0:T(8,128)(2,1)}, u32[]{:S(2)}) copy-start(bf16[2,128,640]{1,2,0:T(8,128)(2,1)} %select_dynamic-update-slice_fusion) | copy-start | bytes 983044
  212.0 10.5 %copy-start.9 = (f32[1,128,1280]{1,2,0:T(8,128)S(1)}, f32[1,128,1280]{1,2,0:T(8,128)}, u32[]{:S(2)}) copy-start(f32[1,128,1280]{1,2,0:T(8,128)} %get-tuple-element.75) | copy-start | bytes 1966084
  212.5 10.9 %copy-start.16 = (bf16[1,2,2,80,128]{4,3,2,1,0:T(8,128)(2,1)S(1)}, bf16[1,2,2,80,128]{4,3,2,1,0:T(8,128)(2,1)}, u32[]{:S(2)}) copy-start(bf16[1,2,2,80,128]{4,3,2,1,0:T(8,128)(2,1)} %copy-done.15) | copy-start | bytes 245764
  212.5 10.9 %copy-start.24 = (bf16[128,160]{0,1:T(8,128)(2,1)S(1)}, bf16[128,160]{0,1:T(8,128)(2,1)}, u32[]{:S(2)}) copy-start(bf16[128,160]{0,1:T(8,128)(2,1)} %convolution_convert_fusion.4) | copy-start | bytes 122884
  212.5 10.9 %copy-start.21 = (bf16[1,2,2,80,128]{4,3,2,1,0:T(8,128)(2,1)S(1)}, bf16[1,2,2,80,128]{4,3,2,1,0:T(8,128)(2,1)}, u32[]{:S(2)}) copy-start(bf16[1,2,2,80,128]{4,3,2,1,0:T(8,128)(2,1)} %copy-done.20) | copy-start | bytes 245764
  223.4 17.8 %copy-start.17 = (bf16[1,2,2,80,128]{4,3,2,1,0:T(8,128)(2,1)}, bf16[1,2,2,80,128]{4,3,2,1,0:T(8,128)(2,1)S(1)}, u32[]{:S(2)}) copy-start(bf16[1,2,2,80,128]{4,3,2,1,0:T(8,128)(2,1)S(1)} %select_dynamic-update-slice_fusion.4) | copy-start | bytes 245764
  223.5 17.7 %copy-start.22 = (bf16[1,2,2,80,128]{4,3,2,1,0:T(8,128)(2,1)}, bf16[1,2,2,80,128]{4,3,2,1,0:T(8,128)(2,1)S(1)}, u32[]{:S(2)}) copy-start(bf16[1,2,2,80,128]{4,3,2,1,0:T(8,128)(2,1)S(1)} %select_dynamic-update-slice_fusion.2) | copy-start | bytes 245764
  (15 other events, 42.8 us)
Sparse Core Ops, SparseCore 0:
  223.5 15.9 all-reduce.1
